TPU v7x, 256 devices: a whole 4x4x8 slice. The times are simulated.
256 devices in a mesh: dp: 32 (over y, z_hi, core), tensor: 8 (over z_lo, x).
Axes of the slice: x: 4, y: 4, z: 8 (z_hi: 4, z_lo: 2; z = z_hi * 2 + z_lo), core: 2. Of those that a mesh axis runs over, the one named last changes fastest.
Arguments:
- inputs: bfloat16 [32768, 2048], P(('dp', 'tensor')), may hold values from -6 to 6
- norm_gain: float32 [2048], replicated, may hold values from 0.1 to 1.9
- proj_weight: bfloat16 [2048, 3, 2048], P('dp', None, 'tensor'), may hold values from -0.125 to 0.125
- filters: float32 [3, 7, 2048], P(None, None, 'tensor'), may hold values from -2.4 to 2.4
- cotangent: bfloat16 [32768, 2048], P('dp', 'tensor'), may hold values from -18 to 18
Outputs:
- mixed: bfloat16 [32768, 2048], P('dp', 'tensor')
- grad_inputs: bfloat16 [32768, 2048], P(('dp', 'tensor'))
- grad_proj: bfloat16 [2048, 3, 2048], P('dp', None, 'tensor')
- grad_filters: float32 [3, 7, 2048], P(None, None, 'tensor')
- grad_gain: float32 [2048], replicated
All inputs are finite; a program needn't handle non-finite values.
Results may differ from a plain program's by a relative error of at most 0.02.
Values may be sent and summed in bfloat16 or wider, within the bound.
No kernel may reach another device: no remote copies, remote signals or barrier semaphores. Data moves between devices by JAX's collectives and lax.ppermute only.
A program may use at most 64 MiB of HBM per device.

v0:
```python
import jax
import jax.numpy as jnp
from jax import lax
from jax.sharding import PartitionSpec as P


def passed_along(shard, axis, by):
    size = lax.axis_size(axis)
    pairs = [(i, i + by) for i in range(size) if 0 <= i + by < size]
    return lax.ppermute(shard, axis, pairs)


def body(inputs, norm_gain, proj_weight, filters, cotangent):
    taps = filters.shape[1]
    width = taps - 1
    wide = inputs.astype(jnp.float32)
    inv_rms = lax.rsqrt(jnp.mean(wide * wide, axis=1, keepdims=True) + 1e-05)
    normed = (wide * inv_rms * norm_gain).astype(jnp.bfloat16)
    weights = lax.all_gather(proj_weight, "dp", axis=0, tiled=True)
    positions = lax.all_gather(normed, "tensor", axis=0, tiled=True)
    length = positions.shape[0]
    streams = jnp.einsum(
        "td,dsc->tsc", positions, weights, preferred_element_type=jnp.float32
    ).astype(jnp.bfloat16)
    before = passed_along(streams[length - width :], "dp", 1)
    extended = jnp.concatenate([before, streams], axis=0).astype(jnp.float32)
    conv = jnp.zeros(streams.shape, jnp.float32)
    for tap in range(taps):
        conv = conv + filters[:, tap, :] * extended[width - tap : width - tap + length]
    mixed = (conv[:, 0] * conv[:, 1] * conv[:, 2]).astype(jnp.bfloat16)
    grad_out = cotangent.astype(jnp.float32)
    grad_conv = jnp.stack(
        [
            grad_out * conv[:, 1] * conv[:, 2],
            grad_out * conv[:, 0] * conv[:, 2],
            grad_out * conv[:, 0] * conv[:, 1],
        ],
        axis=1,
    )
    after = passed_along(grad_conv[:width], "dp", -1)
    grad_extended = jnp.concatenate([grad_conv, after], axis=0)
    grad_acc = jnp.zeros(streams.shape, jnp.float32)
    for tap in range(taps):
        grad_acc = grad_acc + filters[:, tap, :] * grad_extended[tap : tap + length]
    grad_streams = grad_acc.astype(jnp.bfloat16)
    filter_local = jnp.stack(
        [
            jnp.sum(grad_conv * extended[width - tap : width - tap + length], axis=0)
            for tap in range(taps)
        ],
        axis=1,
    )
    normed_terms = jnp.einsum(
        "tsc,dsc->td", grad_streams, weights, preferred_element_type=jnp.float32
    )
    grad_normed = lax.psum_scatter(
        normed_terms.astype(jnp.bfloat16), "tensor", scatter_dimension=0, tiled=True
    ).astype(jnp.float32)
    weight_terms = jnp.einsum(
        "td,tsc->dsc", positions, grad_streams, preferred_element_type=jnp.float32
    )
    grad_proj = lax.psum_scatter(
        weight_terms.astype(jnp.bfloat16), "dp", scatter_dimension=0, tiled=True
    )
    scaled = norm_gain * grad_normed
    grad_inputs = inv_rms * (
        scaled - wide * inv_rms * inv_rms * jnp.mean(scaled * wide, axis=1, keepdims=True)
    )
    gain_local = jnp.sum(grad_normed * wide * inv_rms, axis=0)
    grad_filters = lax.psum(filter_local, "dp")
    grad_gain = lax.psum(gain_local, ("dp", "tensor"))
    return (mixed, grad_inputs.astype(jnp.bfloat16), grad_proj, grad_filters, grad_gain)


def solution(mesh):
    return jax.shard_map(
        body,
        mesh=mesh,
        in_specs=(
            P(("dp", "tensor"), None),
            P(),
            P("dp", None, "tensor"),
            P(None, None, "tensor"),
            P("dp", "tensor"),
        ),
        out_specs=(
            P("dp", "tensor"),
            P(("dp", "tensor"), None),
            P("dp", None, "tensor"),
            P(None, None, "tensor"),
            P(),
        ),
        check_vma=False,
    )
```

profile of v0, /device:TPU:1, one launch (start us, length us, event | category | flops | bytes accessed | tf_op | source)
XLA Modules:
  0.0 393.9 jit_solution(4973453960555978686)
XLA Ops:
  7.2 0.0 all-gather.5.cloned.1.call-start
  7.2 0.7 all-gather.5.cloned.1.call-update
  7.9 0.0 all-gather.3.cloned.1.call-start
  7.9 1.2 fusion.26
  9.2 2.0 fusion.20
  11.2 0.0 all-gather.3.cloned.1.call-update
  11.2 0.0 reduce-scatter.3.cloned.1.call-start
  11.3 1.0 fusion.30
  12.3 59.7 %all-gather.5.cloned.1.call-done = bf16[2048,3,256]{2,0,1:T(8,128)(2,1)} async-done(((bf16[64,3,256]{2,0,1:T(8,128)(2,1)}), bf16[2048,3,256]{2,0,1:T(8,128)(2,1)}) %all-gather.5.cloned.1.call-update) | async-done | bytes 3145744 | tf_op jit(solution)/shard_map/all_gather | solution.py:19
  72.0 54.9 %all-gather.3.cloned.1.call-done = bf16[1024,2048]{1,0:T(8,128)(2,1)} async-done(((bf16[128,2048]{1,0:T(8,128)(2,1)}), bf16[1024,2048]{1,0:T(8,128)(2,1)}) %all-gather.3.cloned.1.call-update) | async-done | bytes 4194320 | tf_op jit(solution)/shard_map/all_gather | solution.py:20
  126.9 6.6 %fusion.14 = bf16[1024,3,256]{2,0,1:T(8,128)(2,1)S(1)} fusion(bf16[2048,3,256]{2,0,1:T(8,128)(2,1)} %all-gather.5.cloned.1.call-done, bf16[1024,2048]{1,0:T(8,128)(2,1)} %all-gather.3.cloned.1.call-done), kind=kOutput, calls=%fused_computation.33 | convolution fusion | flops 3222011904 | bytes 8912896 | tf_op jit(solution)/shard_map/td,dsc->tsc/dot_general | solution.py:22
  133.5 4.7 %collective-permute-start = (bf16[6,3,256]{2,0,1:T(8,128)(2,1)S(1)}, bf16[6,3,256]{2,0,1:T(8,128)(2,1)S(1)}, u32[]{:S(2)}, u32[]{:S(2)}) collective-permute-start(bf16[6,3,256]{2,0,1:T(8,128)(2,1)S(1)} %slice.120), channel_id=1, source_target_pairs={{0,8},{8,16},{16,24},{24,32},{32,40},{40,48},{48,56},{56,64},{64,7... | collective-permute-start | bytes 27656 | tf_op jit(solution)/shard_map/ppermute | solution.py:10
  138.3 0.8 collective-permute-done
  139.1 0.3 maximum_convert_fusion
  139.4 0.0 copy-start.1
  139.4 2.6 multiply_add_fusion
  142.0 0.0 copy-done.1
  142.0 1.2 fusion.25
  143.2 2.9 multiply_reduce_fusion
  146.0 1.9 collective-permute-start.1
  148.0 4.8 %collective-permute-done.1 = f32[6,3,256]{2,0,1:T(8,128)S(1)} collective-permute-done((f32[6,3,256]{2,0,1:T(8,128)S(1)}, f32[6,3,256]{2,0,1:T(8,128)S(1)}, u32[]{:S(2)}, u32[]{:S(2)}) %collective-permute-start.1) | collective-permute-done | bytes 18464 | tf_op jit(solution)/shard_map/ppermute | solution.py:10
  152.8 0.2 pad_maximum_fusion
  153.0 0.0 copy-start.3
  153.0 2.7 fusion.8
  155.8 0.0 copy-done.3
  155.8 5.1 %bitcast_convert_fusion = bf16[1024,2048]{1,0:T(8,128)(2,1)} fusion(bf16[1024,3,256]{2,0,1:T(8,128)(2,1)S(1)} %fusion.8, bf16[2048,3,256]{2,0,1:T(8,128)(2,1)S(1)} %copy-done.3), kind=kOutput, calls=%fused_computation | convolution fusion | flops 3223322624 | bytes 8912896 | tf_op jit(solution)/shard_map/tsc,dsc->td/dot_general | solution.py:53
  160.8 0.0 reduce-scatter.3.cloned.1.call-update
  160.9 0.2 reduce-scatter.5.cloned.1.call-start
  161.1 7.5 %fusion.4 = bf16[2048,3,256]{2,0,1:T(8,128)(2,1)} fusion(bf16[1024,3,256]{2,0,1:T(8,128)(2,1)S(1)} %fusion.8, bf16[1024,2048]{1,0:T(8,128)(2,1)} %all-gather.3.cloned.1.call-done), kind=kOutput, calls=%fused_computation.5 | convolution fusion | flops 3222798336 | bytes 8912896 | tf_op jit(solution)/shard_map/td,tsc->dsc/dot_general | solution.py:59
  168.6 0.0 copy-start
  168.6 0.0 copy-start.2
  168.6 0.0 reduce-scatter.5.cloned.1.call-update
  168.7 135.1 %psum.14 = f32[3,7,256]{2,0,1:T(4,128)S(1)} all-reduce(f32[3,7,256]{2,0,1:T(4,128)S(1)} %constant_dynamic-update-slice_fusion), channel_id=1, replica_groups=mesh['dp'=32,'tensor'=8] {'dp'}, use_global_device_ids=true, to_apply=%region_11.0 | all-reduce | flops 5376 | bytes 43008 | tf_op jit(solution)/shard_map/psum | solution.py:70
  303.8 0.6 copy.12
  304.4 0.0 reduce-scatter.3.cloned.1.call-done
  304.4 0.0 copy-done
  304.5 0.0 copy-done.2
  304.5 1.4 fusion.29
  305.8 79.3 %psum.15 = f32[2048]{0:T(1024)} all-reduce(f32[2048]{0:T(1024)S(1)} %get-tuple-element.17), channel_id=1, replica_groups=mesh['dp'=32,'tensor'=8] {'dp','tensor'}, use_global_device_ids=true, to_apply=%region_13.0 | all-reduce | flops 2048 | bytes 16384 | tf_op jit(solution)/shard_map/psum | solution.py:71
  385.2 2.2 fusion.23
  387.4 0.0 reduce-scatter.5.cloned.1.call-done
  (15 shorter events, 0.1 us)
Async XLA Ops:
  7.2 64.9 %all-gather.5.cloned.1.call-start = ((), (), s32[]{:S(2)}) async-start(), calls=%async_computation.3 | async-start | bytes 3244032 | tf_op jit(solution)/shard_map/all_gather | solution.py:19
  7.9 119.0 %all-gather.3.cloned.1.call-start = ((), (), s32[]{:S(2)}) async-start(), calls=%async_computation.2 | async-start | bytes 4718592 | tf_op jit(solution)/shard_map/all_gather | solution.py:20
  11.2 293.2 %reduce-scatter.3.cloned.1.call-start = ((), (), s32[]{:S(2)}) async-start(), calls=%async_computation.4 | async-start | bytes 4718592 | tf_op jit(solution)/shard_map/reduce_scatter | solution.py:56
  133.5 5.5 %collective-permute-start = (bf16[6,3,256]{2,0,1:T(8,128)(2,1)S(1)}, bf16[6,3,256]{2,0,1:T(8,128)(2,1)S(1)}, u32[]{:S(2)}, u32[]{:S(2)}) collective-permute-start(bf16[6,3,256]{2,0,1:T(8,128)(2,1)S(1)} %slice.120), channel_id=1, source_target_pairs={{0,8},{8,16},{16,24},{24,32},{32,40},{40,48},{48,56},{56,64},{64,7... | collective-permute-start | bytes 27656 | tf_op jit(solution)/shard_map/ppermute | solution.py:10
  139.4 2.6 copy-start.1
  146.0 6.8 %collective-permute-start.1 = (f32[6,3,256]{2,0,1:T(8,128)S(1)}, f32[6,3,256]{2,0,1:T(8,128)S(1)}, u32[]{:S(2)}, u32[]{:S(2)}) collective-permute-start(f32[6,3,256]{2,0,1:T(8,128)S(1)} %slice.131), channel_id=1, source_target_pairs={{8,0},{16,8},{24,16},{32,24},{40,32},{48,40},{56,48},{64,56},{72,6... | collective-permute-start | bytes 55304 | tf_op jit(solution)/shard_map/ppermute | solution.py:10
  153.0 2.7 copy-start.3
  160.9 226.5 %reduce-scatter.5.cloned.1.call-start = ((), (), s32[]{:S(2)}) async-start(), calls=%async_computation.5 | async-start | bytes 3244032 | tf_op jit(solution)/shard_map/reduce_scatter | solution.py:62
  168.6 135.8 %copy-start = (bf16[128,2048]{1,0:T(8,128)(2,1)S(1)}, bf16[128,2048]{1,0:T(8,128)(2,1)}, u32[]{:S(2)}) copy-start(bf16[128,2048]{1,0:T(8,128)(2,1)} %param.5) | copy-start | bytes 1572868
  168.6 135.8 %copy-start.2 = (f32[2048]{0:T(1024)S(1)}, f32[2048]{0:T(1024)}, u32[]{:S(2)}) copy-start(f32[2048]{0:T(1024)} %param.6) | copy-start | bytes 24580
Sparse Core Ops, SparseCore 0:
  10.7 61.3 all-gather.4
  74.4 52.5 all-gather.2
  161.0 54.1 reduce-scatter.2
  219.5 92.7 reduce-scatter.4
where the time goes:
time: 394 us
  blocking collectives  214 us (54%)
  waiting for transfers between devices  121 us (31%)
  matrix products  19.2 us (5%)
  other arithmetic  16.6 us (4%)
  between operations  13.9 us (4%)
  starting transfers between devices  6.99 us (2%)
    psum x1, blocking collectives, body(): grad_filters = lax.psum(filter_local, 'dp')  135 us
    psum x1, blocking collectives, body(): grad_gain = lax.psum(gain_local, ('dp', 'tensor'))  79.3 us
    all_gather x1, waiting for transfers between devices, body(): weights = lax.all_gather(proj_weight, 'dp', axis=0, tiled=True)  59.7 us
    all_gather x1, waiting for transfers between devices, body(): positions = lax.all_gather(normed, 'tensor', axis=0, tiled=True)  54.9 us
  transfers between devices with their start and end apart: 6, of which 4 were waited for; matrix products, arithmetic and copies ran while one was open for 4% of the time, Pallas kernels for 0%

commit v1 on v0

--- a/solution.py
+++ b/solution.py
@@ -68,7 +68,7 @@
     )
     gain_local = jnp.sum(grad_normed * wide * inv_rms, axis=0)
     grad_filters = lax.psum(filter_local, "dp")
-    grad_gain = lax.psum(gain_local, ("dp", "tensor"))
+    grad_gain = lax.psum(lax.psum(gain_local, "dp"), "tensor")
     return (mixed, grad_inputs.astype(jnp.bfloat16), grad_proj, grad_filters, grad_gain)
 
 

time: 394 us -> 386 us (0.980)
  the two profiles are of different devices: /device:TPU:1 before, /device:TPU:32 now
where the time goes in v1:
time: 386 us; the launch traced here: 385 us
  waiting for transfers between devices  168 us (44%)
  blocking collectives  163 us (42%)
  matrix products  19.1 us (5%)
  other arithmetic  16.7 us (4%)
  between operations  13.9 us (4%)
    psum x1, blocking collectives, body(): grad_filters = lax.psum(filter_local, 'dp')  145 us
    all_gather x1, waiting for transfers between devices, body(): weights = lax.all_gather(proj_weight, 'dp', axis=0, tiled=True)  57 us
    all_gather x1, waiting for transfers between devices, body(): positions = lax.all_gather(normed, 'tensor', axis=0, tiled=True)  55.3 us
    reduce_scatter x1, waiting for transfers between devices, body(): lax.psum_scatter(normed_terms.astype(jnp.bfloat16), 'tensor', scatter_dim...  49.9 us
    psum x1, blocking collectives, body(): grad_gain = lax.psum(lax.psum(gain_local, 'dp'), 'tensor')  18 us
  transfers between devices with their start and end apart: 6, of which 5 were waited for; matrix products, arithmetic and copies ran while one was open for 4% of the time, Pallas kernels for 0%

profile of v1, /device:TPU:32, one launch (start us, length us, event | category | flops | bytes accessed | tf_op | source)
XLA Modules:
  0.0 385.2 jit_solution(18349067053917959614)
XLA Ops:
  7.2 0.0 all-gather.5.cloned.1.call-start
  7.2 0.7 all-gather.5.cloned.1.call-update
  7.9 0.0 all-gather.3.cloned.1.call-start
  7.9 1.2 fusion.26
  9.2 2.0 fusion.20
  11.2 0.0 all-gather.3.cloned.1.call-update
  11.2 0.0 reduce-scatter.3.cloned.1.call-start
  11.3 1.0 fusion.30
  12.3 57.0 %all-gather.5.cloned.1.call-done = bf16[2048,3,256]{2,0,1:T(8,128)(2,1)} async-done(((bf16[64,3,256]{2,0,1:T(8,128)(2,1)}), bf16[2048,3,256]{2,0,1:T(8,128)(2,1)}) %all-gather.5.cloned.1.call-update) | async-done | bytes 3145744 | tf_op jit(solution)/shard_map/all_gather | solution.py:19
  69.3 55.3 %all-gather.3.cloned.1.call-done = bf16[1024,2048]{1,0:T(8,128)(2,1)} async-done(((bf16[128,2048]{1,0:T(8,128)(2,1)}), bf16[1024,2048]{1,0:T(8,128)(2,1)}) %all-gather.3.cloned.1.call-update) | async-done | bytes 4194320 | tf_op jit(solution)/shard_map/all_gather | solution.py:20
  124.7 6.6 %fusion.14 = bf16[1024,3,256]{2,0,1:T(8,128)(2,1)S(1)} fusion(bf16[2048,3,256]{2,0,1:T(8,128)(2,1)} %all-gather.5.cloned.1.call-done, bf16[1024,2048]{1,0:T(8,128)(2,1)} %all-gather.3.cloned.1.call-done), kind=kOutput, calls=%fused_computation.33 | convolution fusion | flops 3222011904 | bytes 8912896 | tf_op jit(solution)/shard_map/td,dsc->tsc/dot_general | solution.py:22
  131.3 1.7 collective-permute-start
  133.0 0.8 collective-permute-done
  133.8 0.3 maximum_convert_fusion
  134.1 0.0 copy-start.1
  134.1 2.6 multiply_add_fusion
  136.7 0.0 copy-done.1
  136.8 1.2 fusion.25
  137.9 2.9 multiply_reduce_fusion
  140.8 1.3 collective-permute-start.1
  142.1 4.1 %collective-permute-done.1 = f32[6,3,256]{2,0,1:T(8,128)S(1)} collective-permute-done((f32[6,3,256]{2,0,1:T(8,128)S(1)}, f32[6,3,256]{2,0,1:T(8,128)S(1)}, u32[]{:S(2)}, u32[]{:S(2)}) %collective-permute-start.1) | collective-permute-done | bytes 18464 | tf_op jit(solution)/shard_map/ppermute | solution.py:10
  146.2 0.2 pad_maximum_fusion
  146.4 0.0 copy-start.3
  146.4 2.7 fusion.8
  149.1 0.0 copy-done.3
  149.1 5.1 %bitcast_convert_fusion = bf16[1024,2048]{1,0:T(8,128)(2,1)} fusion(bf16[1024,3,256]{2,0,1:T(8,128)(2,1)S(1)} %fusion.8, bf16[2048,3,256]{2,0,1:T(8,128)(2,1)S(1)} %copy-done.3), kind=kOutput, calls=%fused_computation | convolution fusion | flops 3223322624 | bytes 8912896 | tf_op jit(solution)/shard_map/tsc,dsc->td/dot_general | solution.py:53
  154.2 0.0 reduce-scatter.3.cloned.1.call-update
  154.2 0.2 reduce-scatter.5.cloned.1.call-start
  154.5 7.5 %fusion.4 = bf16[2048,3,256]{2,0,1:T(8,128)(2,1)} fusion(bf16[1024,3,256]{2,0,1:T(8,128)(2,1)S(1)} %fusion.8, bf16[1024,2048]{1,0:T(8,128)(2,1)} %all-gather.3.cloned.1.call-done), kind=kOutput, calls=%fused_computation.5 | convolution fusion | flops 3222798336 | bytes 8912896 | tf_op jit(solution)/shard_map/td,tsc->dsc/dot_general | solution.py:59
  162.0 0.0 copy-start
  162.0 0.0 copy-start.2
  162.0 0.0 reduce-scatter.5.cloned.1.call-update
  162.1 49.9 %reduce-scatter.3.cloned.1.call-done = bf16[128,2048]{1,0:T(8,128)(2,1)} async-done(((bf16[1024,2048]{1,0:T(8,128)(2,1)}), bf16[128,2048]{1,0:T(8,128)(2,1)}) %reduce-scatter.3.cloned.1.call-update) | async-done | bytes 524304 | tf_op jit(solution)/shard_map/reduce_scatter | solution.py:56
  212.0 0.0 copy-done
  212.0 0.0 copy-done.2
  212.0 1.4 fusion.29
  213.4 144.5 %all-reduce = (f32[3,7,256]{2,0,1:T(4,128)S(1)}, f32[2048]{0:T(1024)S(1)}) all-reduce(f32[3,7,256]{2,0,1:T(4,128)S(1)} %constant_dynamic-update-slice_fusion, f32[2048]{0:T(1024)S(1)} %get-tuple-element.17), channel_id=1, replica_groups=mesh['dp'=32,'tensor'=8] {'dp'}, use_global_device_ids=true, to_apply=%region_11.0 | all-reduce | flops 7424 | bytes 59392 | tf_op jit(solution)/shard_map/psum | solution.py:70
  357.9 0.6 copy.12
  358.5 18.0 %psum.23 = f32[2048]{0:T(1024)} all-reduce(f32[2048]{0:T(1024)S(1)} %get-tuple-element.20), channel_id=1, replica_groups=mesh['dp'=32,'tensor'=8] {'tensor'}, use_global_device_ids=true, to_apply=%region_14.0 | all-reduce | flops 2048 | bytes 16384 | tf_op jit(solution)/shard_map/psum | solution.py:71
  376.5 2.2 fusion.23
  378.7 0.0 reduce-scatter.5.cloned.1.call-done
  (15 shorter events, 0.1 us)
Async XLA Ops:
  7.2 62.2 %all-gather.5.cloned.1.call-start = ((), (), s32[]{:S(2)}) async-start(), calls=%async_computation.3 | async-start | bytes 3244032 | tf_op jit(solution)/shard_map/all_gather | solution.py:19
  7.9 116.8 %all-gather.3.cloned.1.call-start = ((), (), s32[]{:S(2)}) async-start(), calls=%async_computation.2 | async-start | bytes 4718592 | tf_op jit(solution)/shard_map/all_gather | solution.py:20
  11.2 200.7 %reduce-scatter.3.cloned.1.call-start = ((), (), s32[]{:S(2)}) async-start(), calls=%async_computation.4 | async-start | bytes 4718592 | tf_op jit(solution)/shard_map/reduce_scatter | solution.py:56
  131.3 2.6 collective-permute-start
  134.1 2.6 copy-start.1
  140.8 5.4 %collective-permute-start.1 = (f32[6,3,256]{2,0,1:T(8,128)S(1)}, f32[6,3,256]{2,0,1:T(8,128)S(1)}, u32[]{:S(2)}, u32[]{:S(2)}) collective-permute-start(f32[6,3,256]{2,0,1:T(8,128)S(1)} %slice.131), channel_id=1, source_target_pairs={{8,0},{16,8},{24,16},{32,24},{40,32},{48,40},{56,48},{64,56},{72,6... | collective-permute-start | bytes 55304 | tf_op jit(solution)/shard_map/ppermute | solution.py:10
  146.4 2.7 copy-start.3
  154.2 224.4 %reduce-scatter.5.cloned.1.call-start = ((), (), s32[]{:S(2)}) async-start(), calls=%async_computation.5 | async-start | bytes 3244032 | tf_op jit(solution)/shard_map/reduce_scatter | solution.py:62
  162.0 50.0 %copy-start = (bf16[128,2048]{1,0:T(8,128)(2,1)S(1)}, bf16[128,2048]{1,0:T(8,128)(2,1)}, u32[]{:S(2)}) copy-start(bf16[128,2048]{1,0:T(8,128)(2,1)} %param.5) | copy-start | bytes 1572868
  162.0 50.0 %copy-start.2 = (f32[2048]{0:T(1024)S(1)}, f32[2048]{0:T(1024)}, u32[]{:S(2)}) copy-start(f32[2048]{0:T(1024)} %param.6) | copy-start | bytes 24580
Sparse Core Ops, SparseCore 0:
  10.7 58.6 all-gather.4
  71.7 52.9 all-gather.2
  154.4 57.5 reduce-scatter.2
  216.3 94.9 reduce-scatter.4
